TPU v7x, 256 devices: a whole 4x4x8 slice. The times are simulated.
256 devices in a mesh: req: 32 (over x, z), kv: 8 (over y, core).
Axes of the slice: x: 4, y: 4, z: 8, core: 2. Of those that a mesh axis runs over, the one named last changes fastest.
Arguments:
- states: bfloat16 [256, 2560], P(('req', 'kv')), may hold values from -6 to 6
- norm_gain: bfloat16 [2560], replicated, may hold values from 0.099609375 to 1.8984375
- w_query: bfloat16 [2560, 2560], P(None, 'kv'), may hold values from -0.125 to 0.125
- key_projection_weight: bfloat16 [2560, 640], P(None, 'kv'), may hold values from -0.125 to 0.125
- value_projection_weight: bfloat16 [2560, 640], P(None, 'kv'), may hold values from -0.125 to 0.125
- cache_keys: bfloat16 [256, 8, 80, 4096], P('req', 'kv')
- value_cache_slots: bfloat16 [256, 8, 80, 4096], P('req', 'kv'), may hold values from -6 to 6
- lengths: int32 [256], P('req'), may hold values from 1 to 16383, as said below
- write_pos: int32 [256], P('req'), may hold values from 0 to 4095, as said below
- dealing: int32 [256], replicated, may hold values from 0 to 255, each once
Outputs:
- context: bfloat16 [256, 2560], P(('req', 'kv'))
Inputs may be any that keep to these rules, and one draw needn't show every extreme that they name: `lengths`: largest value is reached by some request in every draw. write_pos equals lengths modulo 4096. `dealing`: A permutation of the requests.
All inputs are finite; a program needn't handle non-finite values.
Results may differ from a plain program's by a relative error of at most 0.022.
The roundings to bfloat16 on the way count: a program that leaves them out, or rounds other values in their place, can miss the bound.
Values may be sent and summed in bfloat16 or wider, within the bound.
No kernel may reach another device: no remote copies, remote signals or barrier semaphores. Data moves between devices by JAX's collectives and lax.ppermute only.
A program may use at most 64 MiB of HBM per device.

v0:
```python
import jax
import jax.numpy as jnp
from jax import lax
from jax.sharding import PartitionSpec as P

HEAD_DIMENSION = 80


def apply_rotary(tensor, positions):
    half_width = tensor.shape[-1] // 2
    frequency = 10000.0 ** (-(jnp.arange(half_width, dtype=jnp.float32) * 2.0 / tensor.shape[-1]))
    angles = positions.astype(jnp.float32)[:, None] * frequency[None, :]
    cosine = jnp.cos(angles)[:, None, :]
    sine_part = jnp.sin(angles)[:, None, :]
    front_half = tensor[..., :half_width]
    back_half = tensor[..., half_width:]
    return jnp.concatenate(
        [front_half * cosine - back_half * sine_part, back_half * cosine + front_half * sine_part],
        axis=-1,
    )


def local(
    states,
    norm_gain,
    w_query,
    key_projection_weight,
    value_projection_weight,
    cache_keys,
    value_cache_slots,
    lengths,
    write_pos,
    dealing,
):
    kv_count = lax.axis_size("kv")
    per_device = states.shape[0]
    group_rows = per_device * kv_count
    group_index = lax.axis_index("req")
    kv_index = lax.axis_index("kv")
    req_count = lax.axis_size("req")
    dealt_ids = lax.dynamic_slice_in_dim(dealing, group_index * group_rows, group_rows)
    column_rows = lax.all_gather(states, "req", axis=0, tiled=True)
    column_ids = jnp.arange(req_count, dtype=jnp.int32) * kv_count + kv_index
    pick_in = (dealt_ids[:, None] == column_ids[None, :]).astype(jnp.bfloat16)
    own_part = jnp.dot(pick_in, column_rows, preferred_element_type=jnp.float32).astype(
        jnp.bfloat16
    )
    dealt_rows = lax.psum(own_part, "kv")
    wide_rows = dealt_rows.astype(jnp.float32)
    inv_rms = lax.rsqrt(jnp.mean(wide_rows * wide_rows, axis=1, keepdims=True) + 1e-05)
    normalized_input = (wide_rows * inv_rms * norm_gain.astype(jnp.float32)[None, :]).astype(
        jnp.bfloat16
    )
    head_size = HEAD_DIMENSION
    heads_dev = key_projection_weight.shape[1] // head_size
    queries_per_group = w_query.shape[1] // key_projection_weight.shape[1]
    window_size = cache_keys.shape[3]
    query_vectors = jnp.dot(normalized_input, w_query, preferred_element_type=jnp.float32).reshape(
        group_rows, heads_dev * queries_per_group, head_size
    )
    query_vectors = (
        apply_rotary(query_vectors, lengths)
        .astype(jnp.bfloat16)
        .reshape(group_rows, heads_dev, queries_per_group, head_size)
    )
    fresh_key_rows = jnp.dot(
        normalized_input, key_projection_weight, preferred_element_type=jnp.float32
    ).reshape(group_rows, heads_dev, head_size)
    fresh_key_rows = apply_rotary(fresh_key_rows, lengths).astype(jnp.bfloat16)
    fresh_value_rows = (
        jnp.dot(normalized_input, value_projection_weight, preferred_element_type=jnp.float32)
        .astype(jnp.bfloat16)
        .reshape(group_rows, heads_dev, head_size)
    )
    score_scale = 1.0 / head_size**0.5
    scores = (
        jnp.einsum("rkgh,rkhw->rkgw", query_vectors, cache_keys, preferred_element_type=jnp.float32)
        * score_scale
    )
    own_score = (
        jnp.einsum(
            "rkgh,rkh->rkg", query_vectors, fresh_key_rows, preferred_element_type=jnp.float32
        )
        * score_scale
    )
    slot_ids = lax.broadcasted_iota(jnp.int32, (group_rows, 1, 1, window_size), 3)
    at_write = slot_ids == write_pos[:, None, None, None]
    scores = jnp.where(at_write, own_score[..., None], scores)
    scores = jnp.where(slot_ids <= lengths[:, None, None, None], scores, -jnp.inf)
    row_max = jnp.max(scores, axis=-1, keepdims=True)
    expd = jnp.exp(scores - row_max)
    softmax_weights = (expd / jnp.sum(expd, axis=-1, keepdims=True)).astype(jnp.bfloat16)
    stale_weights = jnp.where(at_write, jnp.zeros((), jnp.bfloat16), softmax_weights)
    fresh_weight = jnp.sum(
        jnp.where(at_write, softmax_weights, jnp.zeros((), jnp.bfloat16)).astype(jnp.float32),
        axis=-1,
    )
    mixed = jnp.einsum(
        "rkgw,rkhw->rkgh", stale_weights, value_cache_slots, preferred_element_type=jnp.float32
    )
    mixed = mixed + fresh_weight[..., None] * fresh_value_rows[:, :, None, :].astype(jnp.float32)
    attended = mixed.reshape(group_rows, heads_dev * queries_per_group * head_size).astype(
        jnp.bfloat16
    )
    group_context = lax.all_gather(attended, "kv", axis=1, tiled=True)
    pick_out = (column_ids[:, None] == dealt_ids[None, :]).astype(jnp.bfloat16)
    routed = jnp.dot(pick_out, group_context, preferred_element_type=jnp.float32).astype(
        jnp.bfloat16
    )
    result = lax.psum_scatter(routed, "req", scatter_dimension=0, tiled=True)
    return result


def solution(mesh):
    in_specs = (
        P(("req", "kv"), None),
        P(),
        P(None, "kv"),
        P(None, "kv"),
        P(None, "kv"),
        P("req", "kv", None, None),
        P("req", "kv", None, None),
        P("req"),
        P("req"),
        P(),
    )
    out_specs = P(("req", "kv"), None)
    return jax.shard_map(local, mesh=mesh, in_specs=in_specs, out_specs=out_specs, check_vma=False)
```

profile of v0, /device:TPU:8, one launch (start us, length us, event | category | flops | bytes accessed | tf_op | source)
XLA Modules:
  0.0 262.5 jit_solution(17877185251697256283)
XLA Ops:
  6.5 0.0 copy-start
  6.5 0.0 all-reduce.3.cloned.1.call-start
  6.6 0.8 convert_element_type.54
  7.3 0.7 iota_compare_fusion
  8.1 0.7 convert_element_type.52
  8.8 0.7 iota_compare_fusion.1
  9.5 52.7 %all-gather = bf16[32,1,2560]{2,1,0:T(2,128)(2,1)S(1)} all-gather(bf16[1,1,2560]{2,1,0:T(2,128)(2,1)} %bitcast.43), channel_id=1, replica_groups=mesh['req'=32,'kv'=8] {'req'}, dimensions={0}, use_global_device_ids=true | all-gather | bytes 168960 | tf_op jit(solution)/shard_map/all_gather | solution.py:42
  62.3 0.8 dynamic_slice.3
  63.0 0.2 convolution_convert_fusion.1
  63.2 21.0 %psum.7 = bf16[8,2560]{1,0:T(8,128)(2,1)S(1)} all-reduce(bf16[8,2560]{1,0:T(8,128)(2,1)S(1)} %convolution_convert_fusion.1), channel_id=1, replica_groups=mesh['req'=32,'kv'=8] {'kv'}, use_global_device_ids=true, to_apply=%region_0.0 | all-reduce | flops 20480 | bytes 81920 | tf_op jit(solution)/shard_map/psum | solution.py:48
  84.2 0.1 fusion.28
  84.4 0.1 multiply_cosine_fusion.1
  84.5 1.3 convolution_bitcast_fusion
  85.7 0.1 fusion.48
  85.9 1.3 fusion.22
  87.1 0.0 copy-done
  87.1 0.5 fusion.52
  87.7 0.1 reshape.241
  87.7 0.1 maximum_bitcast_fusion
  87.8 0.1 subtract_convert_fusion
  87.9 0.2 fusion.43
  88.1 0.0 copy-start.1
  88.1 3.7 %fusion.54 = (f32[8,4]{1,0:T(8,128)S(1)}, f32[8,4,4096]{2,1,0:T(4,128)S(1)}) fusion(bf16[8,1,80,4096]{3,2,1,0:T(8,128)(2,1)} %param.15, f32[8,4]{1,0:T(8,128)S(1)} %broadcast_multiply_fusion, pred[8,4096]{1,0:T(8,128)(4,1)S(1)} %iota_compare_fusion, pred[8,4096]{1,0:T(8,128)(4,1)S(1)} %iota_compare_fusion.1, bf16[8,4,40]{2,1,0:T(4,128)(2,1)S(1)} %get-tuple-element.8, ...), kind=kOutput, calls=%fused_computation.64 | convolution fusion | flops 21641216 | bytes 5838080 | tf_op jit(solution)/shard_map/sub | solution.py:91
  91.8 0.4 convert_reduce_fusion
  92.2 4.0 %fusion.19 = bf16[8,4,80]{2,1,0:T(4,128)(2,1)S(1)} fusion(bf16[8,1,80,4096]{3,2,1,0:T(8,128)(2,1)} %param.16, bf16[8,4,4096]{2,1,0:T(4,128)(2,1)S(1)} %get-tuple-element.6, pred[8,4096]{1,0:T(8,128)(4,1)S(1)} %iota_compare_fusion.1, f32[8,80]{1,0:T(8,128)S(1)} %fusion.22, f32[8,4]{1,0:T(8,128)S(1)} %get-tuple-element.5), kind=kOutput, calls=%fused_computation.13 | convolution fusion | flops 21110272 | bytes 5545600 | tf_op jit(solution)/shard_map/rkgw,rkhw->rkgh/dot_general | solution.py:98
  96.1 0.1 convert_element_type.60
  96.2 13.1 %all-gather.1 = bf16[8,320,8]{1,2,0:T(8,128)(2,1)S(1)} all-gather(bf16[1,320,8]{1,2,0:T(8,128)(2,1)S(1)} %bitcast.42), channel_id=1, replica_groups=mesh['req'=32,'kv'=8] {'kv'}, dimensions={0}, use_global_device_ids=true | all-gather | bytes 46080 | tf_op jit(solution)/shard_map/all_gather | solution.py:105
  109.4 0.1 reshape.248
  109.5 0.9 convolution_convert_fusion
  110.4 0.0 all-reduce.3.cloned.1.call-update
  110.4 0.0 copy-done.1
  110.4 0.7 dynamic-slice
  111.1 142.5 %all-reduce.3.cloned.1.call-done = bf16[32,2560]{1,0:T(8,128)(2,1)} async-done(((bf16[32,2560]{1,0:T(8,128)(2,1)}), bf16[32,2560]{1,0:T(8,128)(2,1)}) %all-reduce.3.cloned.1.call-update) | async-done | bytes 163856
  253.6 2.1 constant_dynamic-slice_fusion
  (5 shorter events, 0.0 us)
Async XLA Ops:
  6.5 80.6 %copy-start = (bf16[2560,320]{0,1:T(8,128)(2,1)S(1)}, bf16[2560,320]{0,1:T(8,128)(2,1)}, u32[]{:S(2)}) copy-start(bf16[2560,320]{0,1:T(8,128)(2,1)} %param.12) | copy-start | bytes 4915204
  6.5 247.0 %all-reduce.3.cloned.1.call-start = ((), (), s32[]{:S(2)}) async-start(), calls=%async_computation | async-start | bytes 327680
  88.1 22.3 %copy-start.1 = (u32[256]{0:T(256)S(1)}, u32[256]{0:T(256)}, u32[]{:S(2)}) copy-start(u32[256]{0:T(256)} %constant.44) | copy-start | bytes 3076
Sparse Core Ops, SparseCore 0:
  110.5 142.9 all-reduce.2
where the time goes:
time: 263 us; the launch traced here: 262 us
  waiting for transfers between devices  143 us (54%)
  blocking collectives  86.9 us (33%)
  between operations  13.5 us (5%)
  matrix products  12 us (5%)
  other arithmetic  3.91 us (1%)
  local copies, waits for them, and re-layouts  3.79 us (1%)
    unnamed x2, waiting for transfers between devices  143 us
    all_gather x1, blocking collectives, local(): column_rows = lax.all_gather(states, 'req', axis=0, tiled=True)  52.7 us
    psum x1, blocking collectives, local(): dealt_rows = lax.psum(own_part, 'kv')  21 us
    all_gather x1, blocking collectives, local(): group_context = lax.all_gather(attended, 'kv', axis=1, tiled=True)  13.1 us
  transfers between devices with their start and end apart: 1, of which 1 were waited for; matrix products, arithmetic and copies ran while one was open for 0% of the time, Pallas kernels for 0%

commit v1 on v0

--- a/solution.py
+++ b/solution.py
@@ -45,7 +45,18 @@
     own_part = jnp.dot(pick_in, column_rows, preferred_element_type=jnp.float32).astype(
         jnp.bfloat16
     )
-    dealt_rows = lax.psum(own_part, "kv")
+
+    def wait_state(a_name, buf):
+        chips = lax.axis_size(a_name)
+        parts_out = buf
+        for i in [m for m in (1, 2, 4, 8, 16) if m < chips]:
+            n_now = lax.ppermute(
+                parts_out, axis_name=a_name, perm=[(ix, ix ^ i) for ix in range(chips)]
+            )
+            parts_out = parts_out + n_now
+        return parts_out
+
+    dealt_rows = wait_state("kv", own_part)
     wide_rows = dealt_rows.astype(jnp.float32)
     inv_rms = lax.rsqrt(jnp.mean(wide_rows * wide_rows, axis=1, keepdims=True) + 1e-05)
     normalized_input = (wide_rows * inv_rms * norm_gain.astype(jnp.float32)[None, :]).astype(

time: 263 us -> 249 us (0.947)
  blocking collectives: 86.9 us -> 65.9 us
  starting transfers between devices: 0.01 us -> 3.01 us
  waiting for transfers between devices: 143 us -> 146 us
    psum x1 -> x0, blocking collectives: 21 us -> none  [local(): dealt_rows = lax.psum(own_part, 'kv')]
    ppermute x0 -> x3, waiting for transfers between devices: none -> 5.29 us  [wait_state(): lax.ppermute(parts_out, axis_name=a_name, perm=[(ix, ix ^ i) for ix in ra...]
    ppermute x0 -> x3, starting transfers between devices: none -> 3.01 us  [wait_state(): lax.ppermute(parts_out, axis_name=a_name, perm=[(ix, ix ^ i) for ix in ra...]
  transfers between devices with their start and end apart: 1 -> 4, of which waited for: 1 -> 3; matrix products, arithmetic and copies ran while one was open for 0% -> 1% of each run, Pallas kernels for 0% -> 0%
where the time goes in v1:
time: 249 us; the launch traced here: 248 us
  waiting for transfers between devices  146 us (59%)
  blocking collectives  65.9 us (26%)
  between operations  13.5 us (5%)
  matrix products  11.9 us (5%)
  other arithmetic  3.89 us (2%)
  local copies, waits for them, and re-layouts  3.78 us (2%)
  starting transfers between devices  3.01 us (1%)
    unnamed x2, waiting for transfers between devices  141 us
    all_gather x1, blocking collectives, local(): column_rows = lax.all_gather(states, 'req', axis=0, tiled=True)  52.8 us
    all_gather x1, blocking collectives, local(): group_context = lax.all_gather(attended, 'kv', axis=1, tiled=True)  13 us
    ppermute x3, waiting for transfers between devices, wait_state(): lax.ppermute(parts_out, axis_name=a_name, perm=[(ix, ix ^ i) for ix in ra...  5.29 us
  transfers between devices with their start and end apart: 4, of which 3 were waited for; matrix products, arithmetic and copies ran while one was open for 1% of the time, Pallas kernels for 0%

profile of v1, /device:TPU:8, one launch (start us, length us, event | category | flops | bytes accessed | tf_op | source)
XLA Modules:
  0.0 248.3 jit_solution(791129896298751872)
XLA Ops:
  6.5 0.0 copy-start
  6.5 0.0 all-reduce.3.cloned.1.call-start
  6.5 52.8 %all-gather = bf16[32,1,2560]{2,1,0:T(2,128)(2,1)S(1)} all-gather(bf16[1,1,2560]{2,1,0:T(2,128)(2,1)} %bitcast.46), channel_id=1, replica_groups=mesh['req'=32,'kv'=8] {'req'}, dimensions={0}, use_global_device_ids=true | all-gather | bytes 168960 | tf_op jit(solution)/shard_map/all_gather | solution.py:42
  59.4 0.8 dynamic_slice.3
  60.1 0.2 convolution_convert_fusion.1
  60.3 0.1 collective-permute-start
  60.4 0.7 iota_compare_fusion.1
  61.2 0.7 iota_compare_fusion
  61.9 0.0 collective-permute-done
  62.0 0.5 collective-permute-start.1
  62.5 0.7 convert_element_type.54
  63.2 2.9 %collective-permute-done.1 = bf16[8,2560]{1,0:T(8,128)(2,1)S(1)} collective-permute-done((bf16[8,2560]{1,0:T(8,128)(2,1)S(1)}, bf16[8,2560]{1,0:T(8,128)(2,1)S(1)}, u32[]{:S(2)}, u32[]{:S(2)}) %collective-permute-start.1) | collective-permute-done | bytes 40992 | tf_op jit(solution)/shard_map/ppermute | solution.py:53
  66.1 2.4 collective-permute-start.2
  68.5 0.1 multiply_cosine_fusion.1
  68.6 0.7 convert_element_type.52
  69.3 2.4 collective-permute-done.2
  71.7 0.1 fusion.28
  71.8 0.1 fusion.30
  71.9 1.2 fusion.22
  73.1 1.2 convolution_bitcast_fusion
  74.3 0.0 copy-done
  74.3 0.6 fusion.53
  74.9 0.1 fusion.48
  75.0 0.1 reshape.241
  75.1 0.1 maximum_bitcast_fusion
  75.2 0.1 subtract_convert_fusion
  75.2 0.2 fusion.43
  75.5 0.0 copy-start.1
  75.5 3.7 %fusion.50 = (f32[8,4]{1,0:T(8,128)S(1)}, f32[8,4,4096]{2,1,0:T(4,128)S(1)}) fusion(bf16[8,1,80,4096]{3,2,1,0:T(8,128)(2,1)} %param.15, f32[8,4]{1,0:T(8,128)S(1)} %broadcast_multiply_fusion, pred[8,4096]{1,0:T(8,128)(4,1)S(1)} %iota_compare_fusion, pred[8,4096]{1,0:T(8,128)(4,1)S(1)} %iota_compare_fusion.1, bf16[8,4,40]{2,1,0:T(4,128)(2,1)S(1)} %get-tuple-element.8, ...), kind=kOutput, calls=%fused_computation.63 | convolution fusion | flops 21641216 | bytes 5838080 | tf_op jit(solution)/shard_map/sub | solution.py:102
  79.1 0.4 convert_reduce_fusion
  79.5 4.0 %fusion.19 = bf16[8,4,80]{2,1,0:T(4,128)(2,1)S(1)} fusion(bf16[8,1,80,4096]{3,2,1,0:T(8,128)(2,1)} %param.16, bf16[8,4,4096]{2,1,0:T(4,128)(2,1)S(1)} %get-tuple-element.6, pred[8,4096]{1,0:T(8,128)(4,1)S(1)} %iota_compare_fusion.1, f32[8,80]{1,0:T(8,128)S(1)} %fusion.22, f32[8,4]{1,0:T(8,128)S(1)} %get-tuple-element.5), kind=kOutput, calls=%fused_computation.13 | convolution fusion | flops 21110272 | bytes 5545600 | tf_op jit(solution)/shard_map/rkgw,rkhw->rkgh/dot_general | solution.py:109
  83.5 0.1 convert_element_type.60
  83.6 13.0 %all-gather.1 = bf16[8,320,8]{1,2,0:T(8,128)(2,1)S(1)} all-gather(bf16[1,320,8]{1,2,0:T(8,128)(2,1)S(1)} %bitcast.45), channel_id=1, replica_groups=mesh['req'=32,'kv'=8] {'kv'}, dimensions={0}, use_global_device_ids=true | all-gather | bytes 46080 | tf_op jit(solution)/shard_map/all_gather | solution.py:116
  96.6 0.1 reshape.248
  96.7 0.9 convolution_convert_fusion
  97.6 0.0 all-reduce.3.cloned.1.call-update
  97.6 0.0 copy-done.1
  97.6 0.7 dynamic-slice
  98.3 141.1 %all-reduce.3.cloned.1.call-done = bf16[32,2560]{1,0:T(8,128)(2,1)} async-done(((bf16[32,2560]{1,0:T(8,128)(2,1)}), bf16[32,2560]{1,0:T(8,128)(2,1)}) %all-reduce.3.cloned.1.call-update) | async-done | bytes 163856
  239.4 2.1 constant_dynamic-slice_fusion
  (7 shorter events, 0.1 us)
Async XLA Ops:
  6.5 67.8 %copy-start = (bf16[2560,320]{0,1:T(8,128)(2,1)S(1)}, bf16[2560,320]{0,1:T(8,128)(2,1)}, u32[]{:S(2)}) copy-start(bf16[2560,320]{0,1:T(8,128)(2,1)} %param.12) | copy-start | bytes 4915204
  6.5 232.8 %all-reduce.3.cloned.1.call-start = ((), (), s32[]{:S(2)}) async-start(), calls=%async_computation | async-start | bytes 327680
  60.3 1.6 collective-permute-start
  62.0 4.1 %collective-permute-start.1 = (bf16[8,2560]{1,0:T(8,128)(2,1)S(1)}, bf16[8,2560]{1,0:T(8,128)(2,1)S(1)}, u32[]{:S(2)}, u32[]{:S(2)}) collective-permute-start(bf16[8,2560]{1,0:T(8,128)(2,1)S(1)} %add.49), channel_id=1, source_target_pairs={{0,2},{1,3},{2,0},{3,1},{4,6},{5,7},{6,4},{7,5},{8,10},{9,11},{10,... | collective-permute-start | bytes 122888 | tf_op jit(solution)/shard_map/ppermute | solution.py:53
  66.1 5.6 %collective-permute-start.2 = (bf16[8,2560]{1,0:T(8,128)(2,1)S(1)}, bf16[8,2560]{1,0:T(8,128)(2,1)S(1)}, u32[]{:S(2)}, u32[]{:S(2)}) collective-permute-start(bf16[8,2560]{1,0:T(8,128)(2,1)S(1)} %add.50), channel_id=1, source_target_pairs={{0,4},{1,5},{2,6},{3,7},{4,0},{5,1},{6,2},{7,3},{8,12},{9,13},{10,... | collective-permute-start | bytes 122888 | tf_op jit(solution)/shard_map/ppermute | solution.py:53
  75.5 22.2 %copy-start.1 = (u32[256]{0:T(256)S(1)}, u32[256]{0:T(256)}, u32[]{:S(2)}) copy-start(u32[256]{0:T(256)} %constant.44) | copy-start | bytes 3076
Sparse Core Ops, SparseCore 0:
  97.7 141.6 all-reduce.2
